TPU v7x, 256 devices: a whole 4x4x8 slice. The times are simulated.
256 devices in a mesh: role: 2 (over core), dp: 16 (over x, y), tensor: 8 (over z).
Axes of the slice: x: 4, y: 4, z: 8, core: 2. Of those that a mesh axis runs over, the one named last changes fastest.
Arguments:
- queries: bfloat16 [1024, 128, 576], P(('dp', 'tensor'), 'role'), may hold values from -13 to 13
- latent_cache: bfloat16 [512, 1024, 576], P(('dp', 'tensor')), may hold values from -4 to 4
- new_latent: bfloat16 [1024, 576], P(('dp', 'tensor')), may hold values from -9 to 9
- cache_lengths: int32 [512], P(('dp', 'tensor')), may hold values from 2 to 1024
- value_proj: bfloat16 [128, 512, 128], P(('role', 'tensor')), may hold values from -1 to 1
- out_proj: bfloat16 [16384, 7168], P(('role', 'tensor'), 'dp'), may hold values from -0.046875 to 0.046875
- residual: bfloat16 [1024, 7168], P(('role', 'tensor'), 'dp'), may hold values from -68 to 68
- norm_gain: bfloat16 [7168], replicated, may hold values from 0.5 to 1.5
- routes: int32 [1024, 8], P(('role', 'tensor')), may hold values from 0 to 15, all different within a row; in each aligned block of 64 rows (0 to 63, 64 to 127, ...) at most 40 rows name the same one
- gate_values: float32 [1024, 8], P(('role', 'tensor')), may hold values from 0.2 to 0.8
- tenant_ids: int32 [1024], P(('role', 'tensor')), may hold values from 0 to 2
- expert_gate_weight: bfloat16 [16, 7168, 2048], P('dp', None, ('role', 'tensor')), may hold values from -0.0625 to 0.0625
- expert_up_weight: bfloat16 [16, 7168, 2048], P('dp', None, ('role', 'tensor')), may hold values from -0.0625 to 0.0625
- expert_down_weight: bfloat16 [16, 2048, 7168], P('dp', ('role', 'tensor')), may hold values from -0.125 to 0.125
- left_delta_factor: bfloat16 [3, 16, 2048, 64], P(None, 'dp', ('role', 'tensor')), may hold values from -0.125 to 0.125
- factor_right: bfloat16 [3, 16, 64, 7168], P(None, 'dp'), may hold values from -0.75 to 0.75
Outputs:
- mixed: bfloat16 [1024, 7168], P(('role', 'tensor'), 'dp')
Inputs may be any that keep to these rules, and one draw needn't show every extreme that they name: `routes`: in each aligned block of 64 tokens no expert is named by more than 40 of them.
All inputs are finite; a program needn't handle non-finite values.
Results may differ from a plain program's by a relative error of at most 0.008.
Values may be sent and summed in bfloat16 or wider, within the bound.
No kernel may reach another device: no remote copies, remote signals or barrier semaphores. Data moves between devices by JAX's collectives and lax.ppermute only.
A program may use at most 128 MiB of HBM per device.

v0:
```python
import jax
import jax.numpy as jnp
from jax import lax
from jax.sharding import PartitionSpec as P

LAT = 512
EXPERTS = 16
TEN = 3
SCORE_SCALE = 0.07216878364870323
NORM_EPS = 1e-06
MASKED = -1e30


def rms_rows(input_rows, norm_gain):
    wide = input_rows.astype(jnp.float32)
    scale = lax.rsqrt(jnp.mean(wide * wide, axis=-1, keepdims=True) + NORM_EPS)
    return (wide * scale * norm_gain.astype(jnp.float32)).astype(jnp.bfloat16)


def local(
    queries,
    latent_cache,
    new_latent,
    cache_lengths,
    value_proj,
    out_proj,
    residual,
    norm_gain,
    routes,
    gate_values,
    tenant_ids,
    expert_gate_weight,
    expert_up_weight,
    expert_down_weight,
    left_delta_factor,
    factor_right,
):
    seq_count, context, width = latent_cache.shape
    local_heads = queries.shape[1]
    paired = queries.reshape(seq_count, 2, local_heads, width)
    scores = (
        jnp.einsum("sqhd,spd->sqhp", paired, latent_cache, preferred_element_type=jnp.float32)
        * SCORE_SCALE
    )
    present = jnp.arange(context, dtype=jnp.int32)[None, :] < cache_lengths[:, None]
    scores = jnp.where(present[:, None, None, :], scores, MASKED)
    fresh_keys = new_latent.reshape(seq_count, 2, width)
    fresh = (
        jnp.einsum("sqhd,skd->sqhk", paired, fresh_keys, preferred_element_type=jnp.float32)
        * SCORE_SCALE
    )
    causal = jnp.arange(2)[:, None] >= jnp.arange(2)[None, :]
    fresh = jnp.where(causal[None, :, None, :], fresh, MASKED)
    top = jnp.maximum(jnp.max(scores, axis=3), jnp.max(fresh, axis=3))[..., None]
    weights = jnp.exp(scores - top)
    fresh_weights = jnp.exp(fresh - top)
    total = jnp.sum(weights, axis=3) + jnp.sum(fresh_weights, axis=3)
    summed = jnp.einsum(
        "sqhp,spd->sqhd",
        weights.astype(jnp.bfloat16),
        latent_cache[:, :, :LAT],
        preferred_element_type=jnp.float32,
    )
    summed = summed + jnp.einsum(
        "sqhk,skd->sqhd",
        fresh_weights.astype(jnp.bfloat16),
        fresh_keys[:, :, :LAT],
        preferred_element_type=jnp.float32,
    )
    attended = (
        (summed / total[..., None]).astype(jnp.bfloat16).reshape(seq_count * 2, local_heads, LAT)
    )
    by_head = lax.all_to_all(attended, "tensor", split_axis=1, concat_axis=0, tiled=True)
    head_values = jnp.einsum(
        "thl,hlv->thv", by_head, value_proj, preferred_element_type=jnp.float32
    ).astype(jnp.bfloat16)
    head_values = head_values.reshape(
        head_values.shape[0], head_values.shape[1] * head_values.shape[2]
    )
    all_values = lax.all_gather(head_values, "dp", axis=0, tiled=True)
    group_rows = residual.shape[0]
    input_rows = all_values
    attention = lax.psum_scatter(
        jnp.dot(input_rows, out_proj, preferred_element_type=jnp.float32),
        ("role", "tensor"),
        scatter_dimension=0,
        tiled=True,
    )
    mixed_in = lax.optimization_barrier(
        (residual.astype(jnp.float32) + attention).astype(jnp.bfloat16)
    )
    capacity = 5 * group_rows // 8
    labels = jnp.arange(EXPERTS, dtype=jnp.int32)
    chosen = (routes[:, :, None] == labels[None, None, :]).astype(jnp.int32)
    routed = jnp.sum(chosen, axis=1)
    earlier = jnp.cumsum(routed, axis=0) - routed
    slot_ids = jnp.arange(capacity, dtype=jnp.int32)
    table = (routed.T[:, None, :] > 0) & (earlier.T[:, None, :] == slot_ids[None, :, None])
    local_experts = EXPERTS // lax.axis_size("dp")
    expert_start = lax.axis_index("dp") * local_experts
    mine = lax.dynamic_slice_in_dim(table, expert_start, local_experts, 0)
    full_rows = lax.all_gather(mixed_in, "dp", axis=1, tiled=True)
    picked = jnp.einsum(
        "ecg,gd->ecd", mine.astype(jnp.bfloat16), full_rows, preferred_element_type=jnp.float32
    ).astype(jnp.bfloat16)
    slot_rows = rms_rows(picked, norm_gain)
    slot_owner = jnp.sum(mine.astype(jnp.int32) * tenant_ids[None, None, :], axis=2)
    collected_rows, owners = (
        lax.all_gather(slot_rows, ("role", "tensor"), axis=1, tiled=True),
        lax.all_gather(slot_owner, ("role", "tensor"), axis=1, tiled=True),
    )
    gate_scores = jnp.einsum(
        "gpc,gcb->gpb", collected_rows, expert_gate_weight, preferred_element_type=jnp.float32
    )
    upper_bound = jnp.einsum(
        "gpc,gcb->gpb", collected_rows, expert_up_weight, preferred_element_type=jnp.float32
    )
    hidden = (jax.nn.silu(gate_scores) * upper_bound).astype(jnp.bfloat16)
    owner_mask = (owners[:, :, None] == jnp.arange(TEN, dtype=jnp.int32)[None, None, :]).astype(
        jnp.float32
    )
    widened_right_factor = factor_right.astype(jnp.float32)
    input_rows = hidden
    base_output = jnp.einsum(
        "xog,xgm->oxm", input_rows, expert_down_weight, preferred_element_type=jnp.float32
    )
    mixing_coefficient = (
        jnp.einsum(
            "ywv,oyvh->ywoh", input_rows, left_delta_factor, preferred_element_type=jnp.float32
        )
        * owner_mask[..., None]
    )
    outputs = lax.psum_scatter(
        base_output
        - jnp.einsum(
            "okei,eoiw->kow",
            mixing_coefficient,
            widened_right_factor,
            precision=lax.Precision.HIGHEST,
        ),
        ("role", "tensor"),
        scatter_dimension=0,
        tiled=True,
    ).astype(jnp.bfloat16)
    gate_of = jnp.sum(gate_values[:, :, None] * chosen.astype(jnp.float32), axis=1)
    weighting = table.astype(jnp.float32) * gate_of.T[:, None, :]
    own_weights = lax.dynamic_slice_in_dim(weighting, expert_start, local_experts, 0)
    token_terms = jnp.einsum(
        "lcg,cld->gd", own_weights, outputs.astype(jnp.float32), precision=lax.Precision.HIGHEST
    )
    expert_part = lax.psum_scatter(token_terms, "dp", scatter_dimension=1, tiled=True)
    return (mixed_in.astype(jnp.float32) + expert_part).astype(jnp.bfloat16)


def solution(mesh):
    placed = (
        P(("dp", "tensor"), "role", None),
        P(("dp", "tensor"), None, None),
        P(("dp", "tensor"), None),
        P(("dp", "tensor")),
        P(("role", "tensor"), None, None),
        P(("role", "tensor"), "dp"),
        P(("role", "tensor"), "dp"),
        P(),
        P(("role", "tensor"), None),
        P(("role", "tensor"), None),
        P(("role", "tensor")),
        P("dp", None, ("role", "tensor")),
        P("dp", None, ("role", "tensor")),
        P("dp", ("role", "tensor"), None),
        P(None, "dp", ("role", "tensor"), None),
        P(None, "dp", None, None),
    )
    return jax.shard_map(
        local, mesh=mesh, in_specs=placed, out_specs=P(("role", "tensor"), "dp"), check_vma=False
    )
```

profile of v0, /device:TPU:2, one launch (start us, length us, event | category | flops | bytes accessed | tf_op | source)
XLA Modules:
  0.0 579.4 jit_solution(11137241923393458110)
XLA Ops:
  6.5 0.9 iota_compare_fusion.2
  7.4 0.7 reshape.191
  8.2 3.9 fusion.8
  12.1 0.4 fusion.59
  12.6 0.6 fusion.15
  13.2 2.5 fusion.4
  15.8 1.7 fusion.18
  17.5 0.3 copy.41
  17.8 25.8 %all_to_all.18 = bf16[8,64,512]{2,0,1:T(8,128)(2,1)S(1)} all-to-all(bf16[8,64,512]{2,0,1:T(8,128)(2,1)S(1)} %copy.41), channel_id=1, replica_groups=mesh['role'=2,'dp'=16,'tensor'=8] {'tensor'}, dimensions={1} | all-to-all | bytes 1048576 | tf_op jit(solution)/shard_map/all_to_all | solution.py:73
  43.5 0.3 fusion.25
  43.9 0.7 copy.61
  44.5 0.0 all-gather.6.cloned.1.call-update
  44.6 0.0 reduce-scatter.6.cloned.1.call-start
  44.6 46.0 %all-gather.6.cloned.1.call-done = bf16[1024,1024]{1,0:T(8,128)(2,1)} async-done(((bf16[64,1024]{1,0:T(8,128)(2,1)}), bf16[1024,1024]{1,0:T(8,128)(2,1)}) %all-gather.6.cloned.1.call-update) | async-done | bytes 2097168 | tf_op jit(solution)/shard_map/all_gather | solution.py:80
  90.6 4.4 fusion.60
  95.0 0.0 all-gather.8.cloned.1.call-start
  95.1 0.6 copy-done.7
  95.7 0.1 copy.44
  95.8 0.1 reduce_window_sum.11
  95.9 0.1 copy.46
  96.0 0.1 fusion.37
  96.1 65.1 %reduce-scatter.6.cloned.1.call-done = f32[64,448]{1,0:T(8,128)} async-done(((f32[1024,448]{1,0:T(8,128)}), f32[64,448]{1,0:T(8,128)}) %reduce-scatter.6.cloned.1.call-update) | async-done | bytes 114704 | tf_op jit(solution)/shard_map/reduce_scatter | solution.py:83
  161.2 0.9 add_convert_fusion.1
  162.1 24.2 %all-gather.2 = bf16[16,448,64]{1,2,0:T(8,128)(2,1)S(1)} all-gather(bf16[1,448,64]{1,2,0:T(8,128)(2,1)S(1)} %bitcast.111), channel_id=1, replica_groups=mesh['role'=2,'dp'=16,'tensor'=8] {'dp'}, dimensions={0}, use_global_device_ids=true | all-gather | bytes 974848 | tf_op jit(solution)/shard_map/all_gather | solution.py:102
  186.3 1.6 copy.47
  187.8 2.9 reshape.187
  190.8 1.6 multiply_reduce_fusion
  192.4 1.0 multiply_convert_fusion
  193.4 0.0 all-gather.8.cloned.1.call-update
  193.4 0.0 reduce-scatter.8.cloned.1.call-start
  193.5 0.6 dynamic-slice
  194.7 0.1 select_reduce_fusion
  194.9 0.2 dynamic-update-slice
  195.1 13.6 %all-reduce = s32[640]{0:T(1024)S(1)} all-reduce(s32[640]{0:T(1024)S(1)} %dynamic-update-slice), channel_id=3, replica_groups=mesh['role'=2,'dp'=16,'tensor'=8] {'role','tensor'}, use_global_device_ids=true, to_apply=%add | all-reduce | flops 640 | bytes 5120
  208.7 43.6 %all-gather.8.cloned.1.call-done = bf16[640,7168]{1,0:T(8,128)(2,1)} async-done(((bf16[40,7168]{1,0:T(8,128)(2,1)}), bf16[640,7168]{1,0:T(8,128)(2,1)}) %all-gather.8.cloned.1.call-update) | async-done | bytes 9175056 | tf_op jit(solution)/shard_map/all_gather | solution.py:109
  252.3 6.8 %fusion.13 = f32[640,128]{1,0:T(8,128)S(1)} fusion(bf16[640,7168]{1,0:T(8,128)(2,1)} %all-gather.8.cloned.1.call-done, bf16[1,7168,128]{2,1,0:T(8,128)(2,1)} %param.27), kind=kOutput, calls=%fused_computation.18 | convolution fusion | flops 1174405120 | bytes 11337728 | tf_op jit(solution)/shard_map/gpc,gcb->gpb/dot_general | solution.py:112
  259.1 0.4 copy-done.12
  259.5 2.6 fusion.22
  262.1 8.8 %fusion.9 = f32[640,7168]{1,0:T(8,128)} fusion(bf16[640,128]{1,0:T(8,128)(2,1)S(1)} %fusion.22, bf16[1,128,7168]{2,1,0:T(8,128)(2,1)S(1)} %copy-done.1), kind=kOutput, calls=%fused_computation.14 | convolution fusion | flops 1174405120 | bytes 20348928 | tf_op jit(solution)/shard_map/xog,xgm->oxm/dot_general | solution.py:124
  270.9 0.2 fusion.61
  271.2 14.8 %fusion = f32[640,1,7168]{2,0,1:T(8,128)} fusion(f32[640,7168]{1,0:T(8,128)} %fusion.9, bf16[3,1,64,7168]{3,2,1,0:T(8,128)(2,1)S(1)} %copy-done, f32[640,3,64]{0,2,1:T(8,128)S(1)} %bitcast.107, f32[640,3]{0,1:T(4,128)S(1)} %fusion.47), kind=kOutput, calls=%fused_computation.1 | convolution fusion | flops 10574356480 | bytes 39951872 | tf_op jit(solution)/shard_map/okei,eoiw->kow/dot_general | solution.py:135
  286.0 0.0 reduce-scatter.10.cloned.1.call-start
  286.1 0.6 copy-done.9
  286.7 198.2 %reduce-scatter.8.cloned.1.call-done = f32[40,1,7168]{2,0,1:T(8,128)} async-done(((f32[640,1,7168]{2,0,1:T(8,128)}), f32[40,1,7168]{2,0,1:T(8,128)}) %reduce-scatter.8.cloned.1.call-update) | async-done | bytes 1146896 | tf_op jit(solution)/shard_map/reduce_scatter | solution.py:133
  485.0 5.1 convolution_bitcast_fusion
  490.0 81.2 %reduce-scatter.10.cloned.1.call-done = f32[448,64]{1,0:T(8,128)} async-done(((f32[7168,64]{1,0:T(8,128)}), f32[448,64]{1,0:T(8,128)}) %reduce-scatter.10.cloned.1.call-update) | async-done | bytes 114704
  571.2 1.0 copy.53
  572.3 0.6 add_convert_fusion
  (48 shorter events, 0.3 us)
Async XLA Ops:
  6.5 264.6 %copy-start = (bf16[3,1,64,7168]{3,2,1,0:T(8,128)(2,1)S(1)}, bf16[3,1,64,7168]{3,2,1,0:T(8,128)(2,1)}, u32[]{:S(2)}) copy-start(bf16[3,1,64,7168]{3,2,1,0:T(8,128)(2,1)} %param.31) | copy-start | bytes 8257540
  6.5 84.1 %all-gather.6.cloned.1.call-start = ((), (), s32[]{:S(2)}) async-start(), calls=%async_computation.4 | async-start | bytes 2228224 | tf_op jit(solution)/shard_map/all_gather | solution.py:80
  8.1 5.0 slice-start
  8.1 3.9 copy-start.3
  8.2 5.0 slice-start.1
  13.2 2.6 copy-start.6
  15.8 27.8 %copy-start.2 = (bf16[8,512,128]{2,1,0:T(8,128)(2,1)S(1)}, bf16[8,512,128]{2,1,0:T(8,128)(2,1)}, u32[]{:S(2)}) copy-start(bf16[8,512,128]{2,1,0:T(8,128)(2,1)} %param.20) | copy-start | bytes 3145732
  44.6 116.6 %reduce-scatter.6.cloned.1.call-start = ((), (), s32[]{:S(2)}) async-start(), calls=%async_computation.5 | async-start | bytes 2228224 | tf_op jit(solution)/shard_map/reduce_scatter | solution.py:83
  95.0 0.7 copy-start.7
  95.0 1.0 copy-start.8
  95.0 66.2 %copy-start.4 = (bf16[64,448]{1,0:T(8,128)(2,1)S(1)}, bf16[64,448]{1,0:T(8,128)(2,1)}, u32[]{:S(2)}) copy-start(bf16[64,448]{1,0:T(8,128)(2,1)} %param.22) | copy-start | bytes 172036
  95.0 157.3 %all-gather.8.cloned.1.call-start = ((), (), s32[]{:S(2)}) async-start(), calls=%async_computation.7 | async-start | bytes 9748480 | tf_op jit(solution)/shard_map/all_gather | solution.py:109
  190.8 2.7 copy-start.13
  190.8 4.0 copy-start.10
  193.4 291.5 %reduce-scatter.8.cloned.1.call-start = ((), (), s32[]{:S(2)}) async-start(), calls=%async_computation.6 | async-start | bytes 19496960 | tf_op jit(solution)/shard_map/reduce_scatter | solution.py:133
  252.3 6.8 %copy-start.11 = (bf16[640,7168]{1,0:T(8,128)(2,1)S(1)}, bf16[640,7168]{1,0:T(8,128)(2,1)}, u32[]{:S(2)}) copy-start(bf16[640,7168]{1,0:T(8,128)(2,1)} %all-gather.8.cloned.1.call-done) | copy-start | bytes 27525124
  252.3 7.2 %copy-start.12 = (bf16[1,7168,128]{2,1,0:T(8,128)(2,1)S(1)}, bf16[1,7168,128]{2,1,0:T(8,128)(2,1)}, u32[]{:S(2)}) copy-start(bf16[1,7168,128]{2,1,0:T(8,128)(2,1)} %param.28) | copy-start | bytes 5505028
  259.5 2.6 copy-start.1
  262.1 8.8 %copy-start.5 = (bf16[3,1,128,64]{2,3,1,0:T(8,128)(2,1)S(1)}, bf16[3,1,128,64]{2,3,1,0:T(8,128)(2,1)}, u32[]{:S(2)}) copy-start(bf16[3,1,128,64]{2,3,1,0:T(8,128)(2,1)} %param.30) | copy-start | bytes 147460
  286.0 0.7 copy-start.9
  286.0 285.2 %reduce-scatter.10.cloned.1.call-start = ((), (), s32[]{:S(2)}) async-start(), calls=%async_computation.8 | async-start | bytes 3899392
Sparse Core Ops, SparseCore 0:
  44.7 45.9 all-gather.5
  95.2 65.9 reduce-scatter.5
  193.5 58.7 all-gather.7
  286.1 198.7 reduce-scatter.7
  490.2 80.9 reduce-scatter.9
where the time goes:
time: 580 us; the launch traced here: 579 us
  waiting for transfers between devices  434 us (75%)
  blocking collectives  63.5 us (11%)
  matrix products  53.1 us (9%)
  between operations  14.1 us (2%)
  local copies, waits for them, and re-layouts  9.95 us (2%)
    reduce_scatter x1, waiting for transfers between devices, local(): lax.psum_scatter(base_output - jnp.einsum('okei,eoiw->kow', mixing_coeffi...  198 us
    unnamed x6, waiting for transfers between devices  81.2 us
    reduce_scatter x1, waiting for transfers between devices, local(): lax.psum_scatter(jnp.dot(input_rows, out_proj, preferred_element_type=jnp...  65.1 us
    all_gather x1, waiting for transfers between devices, local(): all_values = lax.all_gather(head_values, 'dp', axis=0, tiled=True)  46 us
    all_gather x1, waiting for transfers between devices, local(): lax.all_gather(slot_rows, ('role', 'tensor'), axis=1, tiled=True)  43.6 us
    all_to_all x1, blocking collectives, local(): lax.all_to_all(attended, 'tensor', split_axis=1, concat_axis=0, tiled=True)  25.8 us
    all_gather x1, blocking collectives, local(): full_rows = lax.all_gather(mixed_in, 'dp', axis=1, tiled=True)  24.2 us
    dot_general x1, matrix products, local(): jnp.einsum('okei,eoiw->kow', mixing_coefficient, widened_right_factor, pr...  14.8 us
  transfers between devices with their start and end apart: 5, of which 5 were waited for; matrix products, arithmetic and copies ran while one was open for 0% of the time, Pallas kernels for 0%

commit v1 on v0

--- a/solution.py
+++ b/solution.py
@@ -77,7 +77,31 @@
     head_values = head_values.reshape(
         head_values.shape[0], head_values.shape[1] * head_values.shape[2]
     )
-    all_values = lax.all_gather(head_values, "dp", axis=0, tiled=True)
+    front = lax.axis_size("dp")
+    z = lax.axis_index("dp")
+    leaves = []
+    moved, small, formed = (front, z, head_values.shape[0])
+    for at, ii in enumerate(head_values.shape):
+        leaves.append(ii * moved if at == 0 else ii)
+    vec_out = jnp.zeros(leaves, head_values.dtype)
+    k_now = val2 = head_values
+    all_values = lax.dynamic_update_slice_in_dim(vec_out, head_values, small * formed, axis=0)
+    for i in range(1, moved // 2 + 1):
+        so_far_all = []
+        for at in range(moved):
+            so_far_all.append((at, (at + 1) % moved))
+        k_now = lax.ppermute(k_now, "dp", so_far_all)
+        all_values = lax.dynamic_update_slice_in_dim(
+            all_values, k_now, (small - i) % moved * formed, axis=0
+        )
+        if 2 * i < moved:
+            arrivals = []
+            for at in range(moved):
+                arrivals.append((at, (at - 1) % moved))
+            val2 = lax.ppermute(val2, "dp", arrivals)
+            all_values = lax.dynamic_update_slice_in_dim(
+                all_values, val2, (small + i) % moved * formed, axis=0
+            )
     group_rows = residual.shape[0]
     input_rows = all_values
     attention = lax.psum_scatter(

time: 580 us -> 594 us (1.024)
  starting transfers between devices: 0.17 us -> 37.9 us
  blocking collectives: 63.5 us -> 37.8 us
    all_gather x1 -> x0, waiting for transfers between devices: 46 us -> none  [local(): all_values = lax.all_gather(head_values, 'dp', axis=0, tiled=True)]
    ppermute x0 -> x15, starting transfers between devices: none -> 29.3 us  [the longest x7 27.6 us: local(): val2 = lax.ppermute(val2, 'dp', arrivals)]
    ppermute x0 -> x15, waiting for transfers between devices: none -> 29 us  [the longest x8 28.9 us: local(): k_now = lax.ppermute(k_now, 'dp', so_far_all)]
    all_to_all x1 -> x0, blocking collectives: 25.8 us -> none  [local(): lax.all_to_all(attended, 'tensor', split_axis=1, concat_axis=0, tiled=True)]
    all_to_all x0 -> x1, waiting for transfers between devices: none -> 17.2 us  [local(): lax.all_to_all(attended, 'tensor', split_axis=1, concat_axis=0, tiled=True)]
    all_to_all x0 -> x1, starting transfers between devices: none -> 8.46 us  [local(): lax.all_to_all(attended, 'tensor', split_axis=1, concat_axis=0, tiled=True)]
    unnamed x6 -> x5, waiting for transfers between devices: 81.2 us -> 81.1 us
  transfers between devices with their start and end apart: 5 -> 20, of which waited for: 5 -> 13; matrix products, arithmetic and copies ran while one was open for 0% -> 0% of each run, Pallas kernels for 0% -> 0%
where the time goes in v1:
time: 594 us; the launch traced here: 593 us
  waiting for transfers between devices  435 us (73%)
  matrix products  52.4 us (9%)
  starting transfers between devices  37.9 us (6%)
  blocking collectives  37.8 us (6%)
  between operations  14.5 us (2%)
  local copies, waits for them, and re-layouts  10.6 us (2%)
    reduce_scatter x1, waiting for transfers between devices, local(): lax.psum_scatter(base_output - jnp.einsum('okei,eoiw->kow', mixing_coeffi...  198 us
    unnamed x5, waiting for transfers between devices  81.1 us
    reduce_scatter x1, waiting for transfers between devices, local(): lax.psum_scatter(jnp.dot(input_rows, out_proj, preferred_element_type=jnp...  66.5 us
    all_gather x1, waiting for transfers between devices, local(): lax.all_gather(slot_rows, ('role', 'tensor'), axis=1, tiled=True)  43.4 us
    ppermute x8, waiting for transfers between devices, local(): k_now = lax.ppermute(k_now, 'dp', so_far_all)  28.9 us
    ppermute x7, starting transfers between devices, local(): val2 = lax.ppermute(val2, 'dp', arrivals)  27.6 us
    all_gather x1, blocking collectives, local(): full_rows = lax.all_gather(mixed_in, 'dp', axis=1, tiled=True)  24.2 us
    all_to_all x1, waiting for transfers between devices, local(): lax.all_to_all(attended, 'tensor', split_axis=1, concat_axis=0, tiled=True)  17.2 us
  transfers between devices with their start and end apart: 20, of which 13 were waited for; matrix products, arithmetic and copies ran while one was open for 0% of the time, Pallas kernels for 0%

profile of v1, /device:TPU:2, one launch (start us, length us, event | category | flops | bytes accessed | tf_op | source)
XLA Modules:
  0.0 593.1 jit_solution(11506151605904056844)
XLA Ops:
  6.5 0.9 iota_compare_fusion.2
  7.4 0.7 reshape.191
  8.2 3.9 fusion.8
  12.6 0.6 fusion.15
  13.2 2.5 fusion.4
  15.8 1.6 fusion.18
  17.4 1.1 copy.41
  18.4 8.5 %all-to-all-start = ((bf16[8,64,512]{2,0,1:T(8,128)(2,1)}), bf16[8,64,512]{2,0,1:T(8,128)(2,1)S(1)}, u32[]{:S(2)}, u32[]{:S(2)}) async-start(bf16[8,64,512]{2,0,1:T(8,128)(2,1)} %copy.41), calls=%async_computation | async-start | bytes 1048576 | tf_op jit(solution)/shard_map/all_to_all | solution.py:73
  27.2 17.2 %all-to-all-done = bf16[8,64,512]{2,0,1:T(8,128)(2,1)S(1)} async-done(((bf16[8,64,512]{2,0,1:T(8,128)(2,1)}), bf16[8,64,512]{2,0,1:T(8,128)(2,1)S(1)}, u32[]{:S(2)}, u32[]{:S(2)}) %all-to-all-start) | async-done | bytes 524320 | tf_op jit(solution)/shard_map/all_to_all | solution.py:73
  44.4 1.5 fusion.25
  46.0 1.6 collective-permute-start
  47.6 2.6 collective-permute-start.1
  50.5 3.1 collective-permute-done
  53.6 4.1 collective-permute-start.3
  57.8 2.9 collective-permute-done.2
  60.7 4.1 collective-permute-start.5
  64.8 2.9 collective-permute-done.4
  67.8 4.1 collective-permute-start.7
  71.9 2.9 collective-permute-done.6
  74.8 4.1 collective-permute-start.9
  79.0 3.6 collective-permute-done.8
  82.6 4.4 collective-permute-start.11
  87.1 3.5 collective-permute-done.10
  90.6 4.1 collective-permute-start.13
  94.8 3.0 collective-permute-done.12
  97.8 7.0 %collective-permute-done.14 = bf16[64,1024]{1,0:T(8,128)(2,1)S(1)} collective-permute-done((bf16[64,1024]{1,0:T(8,128)(2,1)S(1)}, bf16[64,1024]{1,0:T(8,128)(2,1)S(1)}, u32[]{:S(2)}, u32[]{:S(2)}) %collective-permute-start.14) | collective-permute-done | bytes 131104 | tf_op jit(solution)/shard_map/ppermute | solution.py:93
  104.9 2.6 fusion.60
  107.6 0.6 copy-done.6
  108.6 66.5 %reduce-scatter.6.cloned.1.call-done = f32[64,448]{1,0:T(8,128)} async-done(((f32[1024,448]{1,0:T(8,128)}), f32[64,448]{1,0:T(8,128)}) %reduce-scatter.6.cloned.1.call-update) | async-done | bytes 114704 | tf_op jit(solution)/shard_map/reduce_scatter | solution.py:107
  175.1 0.9 add_convert_fusion.1
  176.0 24.2 %all-gather.2 = bf16[16,448,64]{1,2,0:T(8,128)(2,1)S(1)} all-gather(bf16[1,448,64]{1,2,0:T(8,128)(2,1)S(1)} %bitcast.113), channel_id=1, replica_groups=mesh['role'=2,'dp'=16,'tensor'=8] {'dp'}, dimensions={0}, use_global_device_ids=true | all-gather | bytes 974848 | tf_op jit(solution)/shard_map/all_gather | solution.py:126
  200.2 1.6 copy.47
  201.8 2.9 reshape.187
  204.7 1.6 multiply_reduce_fusion
  206.3 1.0 multiply_convert_fusion
  207.4 0.6 dynamic-slice
  209.0 13.6 %all-reduce = s32[640]{0:T(1024)S(1)} all-reduce(s32[640]{0:T(1024)S(1)} %dynamic-update-slice), channel_id=3, replica_groups=mesh['role'=2,'dp'=16,'tensor'=8] {'role','tensor'}, use_global_device_ids=true, to_apply=%add | all-reduce | flops 640 | bytes 5120
  222.6 43.4 %all-gather.5.cloned.1.call-done = bf16[640,7168]{1,0:T(8,128)(2,1)} async-done(((bf16[40,7168]{1,0:T(8,128)(2,1)}), bf16[640,7168]{1,0:T(8,128)(2,1)}) %all-gather.5.cloned.1.call-update) | async-done | bytes 9175056 | tf_op jit(solution)/shard_map/all_gather | solution.py:133
  266.0 6.8 %fusion.13 = f32[640,128]{1,0:T(8,128)S(1)} fusion(bf16[640,7168]{1,0:T(8,128)(2,1)} %all-gather.5.cloned.1.call-done, bf16[1,7168,128]{2,1,0:T(8,128)(2,1)} %param.27), kind=kOutput, calls=%fused_computation.18 | convolution fusion | flops 1174405120 | bytes 11337728 | tf_op jit(solution)/shard_map/gpc,gcb->gpb/dot_general | solution.py:136
  273.3 2.6 fusion.22
  275.8 8.8 %fusion.9 = f32[640,7168]{1,0:T(8,128)} fusion(bf16[640,128]{1,0:T(8,128)(2,1)S(1)} %fusion.22, bf16[1,128,7168]{2,1,0:T(8,128)(2,1)S(1)} %copy-done.1), kind=kOutput, calls=%fused_computation.14 | convolution fusion | flops 1174405120 | bytes 20348928 | tf_op jit(solution)/shard_map/xog,xgm->oxm/dot_general | solution.py:148
  284.9 14.8 %fusion = f32[640,1,7168]{2,0,1:T(8,128)} fusion(f32[640,7168]{1,0:T(8,128)} %fusion.9, bf16[3,1,64,7168]{3,2,1,0:T(8,128)(2,1)S(1)} %copy-done, f32[640,3,64]{0,2,1:T(8,128)S(1)} %bitcast.109, f32[640,3]{0,1:T(4,128)S(1)} %fusion.47), kind=kOutput, calls=%fused_computation.1 | convolution fusion | flops 10574356480 | bytes 39951872 | tf_op jit(solution)/shard_map/okei,eoiw->kow/dot_general | solution.py:159
  299.8 0.6 copy-done.8
  300.4 198.2 %reduce-scatter.8.cloned.1.call-done = f32[40,1,7168]{2,0,1:T(8,128)} async-done(((f32[640,1,7168]{2,0,1:T(8,128)}), f32[40,1,7168]{2,0,1:T(8,128)}) %reduce-scatter.8.cloned.1.call-update) | async-done | bytes 1146896 | tf_op jit(solution)/shard_map/reduce_scatter | solution.py:157
  498.7 5.1 convolution_bitcast_fusion
  503.8 81.1 %reduce-scatter.10.cloned.1.call-done = f32[448,64]{1,0:T(8,128)} async-done(((f32[7168,64]{1,0:T(8,128)}), f32[448,64]{1,0:T(8,128)}) %reduce-scatter.10.cloned.1.call-update) | async-done | bytes 114704
  584.8 1.0 copy.53
  585.9 0.6 add_convert_fusion
  (93 shorter events, 2.8 us)
Async XLA Ops:
  6.5 278.4 %copy-start = (bf16[3,1,64,7168]{3,2,1,0:T(8,128)(2,1)S(1)}, bf16[3,1,64,7168]{3,2,1,0:T(8,128)(2,1)}, u32[]{:S(2)}) copy-start(bf16[3,1,64,7168]{3,2,1,0:T(8,128)(2,1)} %param.31) | copy-start | bytes 8257540
  8.1 5.0 slice-start
  8.1 4.0 copy-start.2
  8.2 5.0 slice-start.1
  13.2 2.5 copy-start.5
  18.4 26.0 %all-to-all-start = ((bf16[8,64,512]{2,0,1:T(8,128)(2,1)}), bf16[8,64,512]{2,0,1:T(8,128)(2,1)S(1)}, u32[]{:S(2)}, u32[]{:S(2)}) async-start(bf16[8,64,512]{2,0,1:T(8,128)(2,1)} %copy.41), calls=%async_computation | async-start | bytes 1048576 | tf_op jit(solution)/shard_map/all_to_all | solution.py:73
  26.9 148.2 %reduce-scatter.6.cloned.1.call-start = ((), (), s32[]{:S(2)}) async-start(), calls=%async_computation.4 | async-start | bytes 2228224 | tf_op jit(solution)/shard_map/reduce_scatter | solution.py:107
  46.0 7.6 %collective-permute-start = (bf16[64,1024]{1,0:T(8,128)(2,1)S(1)}, bf16[64,1024]{1,0:T(8,128)(2,1)S(1)}, u32[]{:S(2)}, u32[]{:S(2)}) collective-permute-start(bf16[64,1024]{1,0:T(8,128)(2,1)S(1)} %bitcast.116), channel_id=1, source_target_pairs={{0,8},{8,16},{16,24},{24,32},{32,40},{40,48},{48,56},{56,64},{64,7... | collective-permute-start | bytes 393224 | tf_op jit(solution)/shard_map/ppermute | solution.py:93
  47.6 6.0 %collective-permute-start.1 = (bf16[64,1024]{1,0:T(8,128)(2,1)S(1)}, bf16[64,1024]{1,0:T(8,128)(2,1)S(1)}, u32[]{:S(2)}, u32[]{:S(2)}) collective-permute-start(bf16[64,1024]{1,0:T(8,128)(2,1)S(1)} %bitcast.117), channel_id=1, source_target_pairs={{0,120},{8,0},{16,8},{24,16},{32,24},{40,32},{48,40},{56,48},{64,5... | collective-permute-start | bytes 393224 | tf_op jit(solution)/shard_map/ppermute | solution.py:101
  50.5 54.4 %copy-start.12 = (bf16[1024,448]{0,1:T(8,128)(2,1)S(1)}, bf16[1024,448]{0,1:T(8,128)(2,1)}, u32[]{:S(2)}) copy-start(bf16[1024,448]{0,1:T(8,128)(2,1)} %param.21) | copy-start | bytes 2752516
  53.6 7.1 %collective-permute-start.2 = (bf16[64,1024]{1,0:T(8,128)(2,1)S(1)}, bf16[64,1024]{1,0:T(8,128)(2,1)S(1)}, u32[]{:S(2)}, u32[]{:S(2)}) collective-permute-start(bf16[64,1024]{1,0:T(8,128)(2,1)S(1)} %collective-permute-done), channel_id=1, source_target_pairs={{0,8},{8,16},{16,24},{24,32},{32,40},{40,48},{48,56},{56,64},{64,7... | collective-permute-start | bytes 393224 | tf_op jit(solution)/shard_map/ppermute | solution.py:93
  53.6 7.1 %collective-permute-start.3 = (bf16[64,1024]{1,0:T(8,128)(2,1)S(1)}, bf16[64,1024]{1,0:T(8,128)(2,1)S(1)}, u32[]{:S(2)}, u32[]{:S(2)}) collective-permute-start(bf16[64,1024]{1,0:T(8,128)(2,1)S(1)} %collective-permute-done.1), channel_id=1, source_target_pairs={{0,120},{8,0},{16,8},{24,16},{32,24},{40,32},{48,40},{56,48},{64,5... | collective-permute-start | bytes 393224 | tf_op jit(solution)/shard_map/ppermute | solution.py:101
  60.7 7.1 %collective-permute-start.4 = (bf16[64,1024]{1,0:T(8,128)(2,1)S(1)}, bf16[64,1024]{1,0:T(8,128)(2,1)S(1)}, u32[]{:S(2)}, u32[]{:S(2)}) collective-permute-start(bf16[64,1024]{1,0:T(8,128)(2,1)S(1)} %collective-permute-done.2), channel_id=1, source_target_pairs={{0,8},{8,16},{16,24},{24,32},{32,40},{40,48},{48,56},{56,64},{64,7... | collective-permute-start | bytes 393224 | tf_op jit(solution)/shard_map/ppermute | solution.py:93
  60.7 7.1 %collective-permute-start.5 = (bf16[64,1024]{1,0:T(8,128)(2,1)S(1)}, bf16[64,1024]{1,0:T(8,128)(2,1)S(1)}, u32[]{:S(2)}, u32[]{:S(2)}) collective-permute-start(bf16[64,1024]{1,0:T(8,128)(2,1)S(1)} %collective-permute-done.3), channel_id=1, source_target_pairs={{0,120},{8,0},{16,8},{24,16},{32,24},{40,32},{48,40},{56,48},{64,5... | collective-permute-start | bytes 393224 | tf_op jit(solution)/shard_map/ppermute | solution.py:101
  67.7 7.1 %collective-permute-start.6 = (bf16[64,1024]{1,0:T(8,128)(2,1)S(1)}, bf16[64,1024]{1,0:T(8,128)(2,1)S(1)}, u32[]{:S(2)}, u32[]{:S(2)}) collective-permute-start(bf16[64,1024]{1,0:T(8,128)(2,1)S(1)} %collective-permute-done.4), channel_id=1, source_target_pairs={{0,8},{8,16},{16,24},{24,32},{32,40},{40,48},{48,56},{56,64},{64,7... | collective-permute-start | bytes 393224 | tf_op jit(solution)/shard_map/ppermute | solution.py:93
  67.8 7.1 %collective-permute-start.7 = (bf16[64,1024]{1,0:T(8,128)(2,1)S(1)}, bf16[64,1024]{1,0:T(8,128)(2,1)S(1)}, u32[]{:S(2)}, u32[]{:S(2)}) collective-permute-start(bf16[64,1024]{1,0:T(8,128)(2,1)S(1)} %collective-permute-done.5), channel_id=1, source_target_pairs={{0,120},{8,0},{16,8},{24,16},{32,24},{40,32},{48,40},{56,48},{64,5... | collective-permute-start | bytes 393224 | tf_op jit(solution)/shard_map/ppermute | solution.py:101
  74.8 7.8 %collective-permute-start.8 = (bf16[64,1024]{1,0:T(8,128)(2,1)S(1)}, bf16[64,1024]{1,0:T(8,128)(2,1)S(1)}, u32[]{:S(2)}, u32[]{:S(2)}) collective-permute-start(bf16[64,1024]{1,0:T(8,128)(2,1)S(1)} %collective-permute-done.6), channel_id=1, source_target_pairs={{0,8},{8,16},{16,24},{24,32},{32,40},{40,48},{48,56},{56,64},{64,7... | collective-permute-start | bytes 393224 | tf_op jit(solution)/shard_map/ppermute | solution.py:93
  74.8 7.8 %collective-permute-start.9 = (bf16[64,1024]{1,0:T(8,128)(2,1)S(1)}, bf16[64,1024]{1,0:T(8,128)(2,1)S(1)}, u32[]{:S(2)}, u32[]{:S(2)}) collective-permute-start(bf16[64,1024]{1,0:T(8,128)(2,1)S(1)} %collective-permute-done.7), channel_id=1, source_target_pairs={{0,120},{8,0},{16,8},{24,16},{32,24},{40,32},{48,40},{56,48},{64,5... | collective-permute-start | bytes 393224 | tf_op jit(solution)/shard_map/ppermute | solution.py:101
  82.6 8.0 %collective-permute-start.10 = (bf16[64,1024]{1,0:T(8,128)(2,1)S(1)}, bf16[64,1024]{1,0:T(8,128)(2,1)S(1)}, u32[]{:S(2)}, u32[]{:S(2)}) collective-permute-start(bf16[64,1024]{1,0:T(8,128)(2,1)S(1)} %collective-permute-done.8), channel_id=1, source_target_pairs={{0,8},{8,16},{16,24},{24,32},{32,40},{40,48},{48,56},{56,64},{64,7... | collective-permute-start | bytes 393224 | tf_op jit(solution)/shard_map/ppermute | solution.py:93
  82.6 8.0 %collective-permute-start.11 = (bf16[64,1024]{1,0:T(8,128)(2,1)S(1)}, bf16[64,1024]{1,0:T(8,128)(2,1)S(1)}, u32[]{:S(2)}, u32[]{:S(2)}) collective-permute-start(bf16[64,1024]{1,0:T(8,128)(2,1)S(1)} %collective-permute-done.9), channel_id=1, source_target_pairs={{0,120},{8,0},{16,8},{24,16},{32,24},{40,32},{48,40},{56,48},{64,5... | collective-permute-start | bytes 393224 | tf_op jit(solution)/shard_map/ppermute | solution.py:101
  90.6 7.1 %collective-permute-start.12 = (bf16[64,1024]{1,0:T(8,128)(2,1)S(1)}, bf16[64,1024]{1,0:T(8,128)(2,1)S(1)}, u32[]{:S(2)}, u32[]{:S(2)}) collective-permute-start(bf16[64,1024]{1,0:T(8,128)(2,1)S(1)} %collective-permute-done.10), channel_id=1, source_target_pairs={{0,8},{8,16},{16,24},{24,32},{32,40},{40,48},{48,56},{56,64},{64,7... | collective-permute-start | bytes 393224 | tf_op jit(solution)/shard_map/ppermute | solution.py:93
  90.6 7.2 %collective-permute-start.13 = (bf16[64,1024]{1,0:T(8,128)(2,1)S(1)}, bf16[64,1024]{1,0:T(8,128)(2,1)S(1)}, u32[]{:S(2)}, u32[]{:S(2)}) collective-permute-start(bf16[64,1024]{1,0:T(8,128)(2,1)S(1)} %collective-permute-done.11), channel_id=1, source_target_pairs={{0,120},{8,0},{16,8},{24,16},{32,24},{40,32},{48,40},{56,48},{64,5... | collective-permute-start | bytes 393224 | tf_op jit(solution)/shard_map/ppermute | solution.py:101
  97.8 7.1 %collective-permute-start.14 = (bf16[64,1024]{1,0:T(8,128)(2,1)S(1)}, bf16[64,1024]{1,0:T(8,128)(2,1)S(1)}, u32[]{:S(2)}, u32[]{:S(2)}) collective-permute-start(bf16[64,1024]{1,0:T(8,128)(2,1)S(1)} %collective-permute-done.12), channel_id=1, source_target_pairs={{0,8},{8,16},{16,24},{24,32},{32,40},{40,48},{48,56},{56,64},{64,7... | collective-permute-start | bytes 393224 | tf_op jit(solution)/shard_map/ppermute | solution.py:93
  107.5 0.7 copy-start.6
  107.5 1.0 copy-start.7
  107.5 67.6 %copy-start.3 = (bf16[64,448]{1,0:T(8,128)(2,1)S(1)}, bf16[64,448]{1,0:T(8,128)(2,1)}, u32[]{:S(2)}) copy-start(bf16[64,448]{1,0:T(8,128)(2,1)} %param.22) | copy-start | bytes 172036
  107.5 158.5 %all-gather.5.cloned.1.call-start = ((), (), s32[]{:S(2)}) async-start(), calls=%async_computation.6 | async-start | bytes 9748480 | tf_op jit(solution)/shard_map/all_gather | solution.py:133
  204.7 2.7 copy-start.13
  204.7 3.9 copy-start.9
  207.3 291.3 %reduce-scatter.8.cloned.1.call-start = ((), (), s32[]{:S(2)}) async-start(), calls=%async_computation.5 | async-start | bytes 19496960 | tf_op jit(solution)/shard_map/reduce_scatter | solution.py:157
  266.0 6.8 %copy-start.10 = (bf16[640,7168]{1,0:T(8,128)(2,1)S(1)}, bf16[640,7168]{1,0:T(8,128)(2,1)}, u32[]{:S(2)}) copy-start(bf16[640,7168]{1,0:T(8,128)(2,1)} %all-gather.5.cloned.1.call-done) | copy-start | bytes 27525124
  266.0 7.2 %copy-start.11 = (bf16[1,7168,128]{2,1,0:T(8,128)(2,1)S(1)}, bf16[1,7168,128]{2,1,0:T(8,128)(2,1)}, u32[]{:S(2)}) copy-start(bf16[1,7168,128]{2,1,0:T(8,128)(2,1)} %param.28) | copy-start | bytes 5505028
  273.3 2.6 copy-start.1
  275.8 8.8 %copy-start.4 = (bf16[3,1,128,64]{2,3,1,0:T(8,128)(2,1)S(1)}, bf16[3,1,128,64]{2,3,1,0:T(8,128)(2,1)}, u32[]{:S(2)}) copy-start(bf16[3,1,128,64]{2,3,1,0:T(8,128)(2,1)} %param.30) | copy-start | bytes 147460
  299.7 0.7 copy-start.8
  299.7 285.1 %reduce-scatter.10.cloned.1.call-start = ((), (), s32[]{:S(2)}) async-start(), calls=%async_computation.7 | async-start | bytes 3899392
Sparse Core Ops, SparseCore 0:
  107.7 67.4 reduce-scatter.5
  207.4 58.5 all-gather.4
  299.8 198.7 reduce-scatter.7
  503.9 80.9 reduce-scatter.9
